TPU v7x, 32 devices: a whole 2x2x4 slice. The times are simulated.
32 devices in a mesh: dp: 8 (over y, x, core), tensor: 4 (over z).
Axes of the slice: x: 2, y: 2, z: 4, core: 2. Of those that a mesh axis runs over, the one named last changes fastest.
Arguments:
- grad_out: bfloat16 [2048, 4096], P('dp'), may hold values from -1.5 to 1.5
- gate_input: bfloat16 [2048, 14336], P('dp', 'tensor'), may hold values from -6 to 6
- up_input: bfloat16 [2048, 14336], P('dp', 'tensor'), may hold values from -6 to 6
- next_hidden: bfloat16 [2048, 14336], P('dp', 'tensor'), may hold values from -6 to 6
- down_weight: bfloat16 [4096, 14336], P(None, 'tensor'), may hold values from -0.046875 to 0.046875
- first_moment: float32 [4096, 14336], P('dp', 'tensor'), may hold values from -48 to 48
- second_moment: float32 [4096, 14336], P('dp', 'tensor'), may hold values from 10 to 200
Outputs:
- gate_grad: bfloat16 [2048, 14336], P('dp', 'tensor')
- up_grad: bfloat16 [2048, 14336], P('dp', 'tensor')
- moment_one: float32 [4096, 14336], P('dp', 'tensor')
- moment_two: float32 [4096, 14336], P('dp', 'tensor')
- next_out: bfloat16 [2048, 4096], P('dp', 'tensor')
All inputs are finite; a program needn't handle non-finite values.
Results may differ from a plain program's by a relative error of at most 0.004.
The roundings to bfloat16 on the way count: a program that leaves them out, or rounds other values in their place, can miss the bound.
Values may be sent and summed in bfloat16 or wider, within the bound.
No kernel may reach another device: no remote copies, remote signals or barrier semaphores. Data moves between devices by JAX's collectives and lax.ppermute only.
A program may use at most 256 MiB of HBM per device.

v0:
```python
import jax
import jax.numpy as jnp
from jax import lax
from jax.sharding import PartitionSpec as P

STEP = 20
beta_one = 0.9
beta_two = 0.95
learn_rate = 0.001
decay_rate = 0.1
epsilon = 1e-08


def shards(grad_out, gate_input, up_input, next_hidden, down_weight, first_moment, second_moment):
    n_dp = lax.axis_size("dp")
    n_t = lax.axis_size("tensor")
    me = lax.axis_index("dp")
    col = lax.axis_index("tensor")
    tok = grad_out.shape[0]
    owned_rows = first_moment.shape[0]
    group = n_dp // n_t
    gate_value = gate_input.astype(jnp.float32)
    up_value = up_input.astype(jnp.float32)
    sigmoid_gate = jax.nn.sigmoid(gate_value)
    activated = gate_value * sigmoid_gate
    hidden = (activated * up_value).astype(jnp.bfloat16)
    hidden_all = lax.all_gather(hidden, "dp", axis=0, tiled=True)
    next_all = lax.all_gather(next_hidden, "dp", axis=0, tiled=True)
    grad_rows = lax.all_to_all(grad_out.T, "dp", 0, 1, tiled=True)
    grad_hidden = jnp.dot(grad_out, down_weight, preferred_element_type=jnp.float32)
    gate_grad = (
        grad_hidden * up_value * sigmoid_gate * (1.0 + gate_value * (1.0 - sigmoid_gate))
    ).astype(jnp.bfloat16)
    up_grad = (grad_hidden * activated).astype(jnp.bfloat16)
    weight_grad = jnp.zeros((owned_rows, hidden.shape[1]), jnp.float32)
    for b in range(n_dp):
        block = jnp.dot(
            grad_rows[:, b * tok : (b + 1) * tok],
            hidden_all[b * tok : (b + 1) * tok],
            preferred_element_type=jnp.float32,
        ).astype(jnp.bfloat16)
        weight_grad = weight_grad + block.astype(jnp.float32)
    moment_one = beta_one * first_moment + (1.0 - beta_one) * weight_grad
    moment_two = beta_two * second_moment + (1.0 - beta_two) * weight_grad * weight_grad
    corrected_one = moment_one / (1.0 - beta_one**STEP)
    corrected_two = moment_two / (1.0 - beta_two**STEP)
    old_shard = lax.dynamic_slice_in_dim(down_weight, me * owned_rows, owned_rows, 0).astype(
        jnp.float32
    )
    new_shard = (
        old_shard
        - learn_rate
        * (corrected_one / (jnp.sqrt(corrected_two) + epsilon) + decay_rate * old_shard)
    ).astype(jnp.bfloat16)
    partial_out = lax.dot_general(
        new_shard, next_all, (((1,), (1,)), ((), ())), preferred_element_type=jnp.float32
    )
    summed = (
        lax.psum_scatter(partial_out, "tensor", scatter_dimension=1, tiled=True)
        .astype(jnp.bfloat16)
        .T
    )
    sub = me % group
    pieces = []
    for k in range(group):
        s = (sub + k) % group
        piece = lax.dynamic_slice_in_dim(summed, s * tok, tok, 0)
        perm = []
        for i in range(n_dp):
            for j in range(n_t):
                si = (i % group + k) % group
                dst = (group * j + si) * n_t + i // group
                perm.append((i * n_t + j, dst))
        pieces.append(lax.ppermute(piece, ("dp", "tensor"), perm))
    ordered = []
    for r in range(group):
        chosen = pieces[0]
        for k in range(1, group):
            chosen = jnp.where((sub - k) % group == r, pieces[k], chosen)
        ordered.append(chosen)
    next_out = jnp.concatenate(ordered, axis=1)
    return (gate_grad, up_grad, moment_one, moment_two, next_out)


def solution(mesh):
    n_dp = mesh.shape["dp"]
    n_t = mesh.shape["tensor"]
    if n_dp % n_t:
        raise ValueError("bad mesh")
    placed = (
        P("dp", None),
        P("dp", "tensor"),
        P("dp", "tensor"),
        P("dp", "tensor"),
        P(None, "tensor"),
        P("dp", "tensor"),
        P("dp", "tensor"),
    )
    return jax.shard_map(
        shards,
        mesh=mesh,
        in_specs=placed,
        out_specs=(
            P("dp", "tensor"),
            P("dp", "tensor"),
            P("dp", "tensor"),
            P("dp", "tensor"),
            P("dp", "tensor"),
        ),
        check_vma=False,
    )
```

profile of v0, /device:TPU:3, one launch (start us, length us, event | category | flops | bytes accessed | tf_op | source)
XLA Modules:
  0.0 363.5 jit_solution(1253085345670090751)
XLA Ops:
  7.2 21.4 %multiply_convert_fusion = (bf16[256,3584]{1,0:T(8,128)(2,1)}, bf16[256,3584]{1,0:T(8,128)(2,1)}, bf16[256,3584]{1,0:T(8,128)(2,1)}) fusion(bf16[256,3584]{1,0:T(8,128)(2,1)} %param.8, bf16[256,3584]{1,0:T(8,128)(2,1)} %param.9, bf16[256,4096]{1,0:T(8,128)(2,1)} %param.7, bf16[4096,3584]{1,0:T(8,128)(2,1)} %param.11), kind=kOutput, calls=%fused_computation.31 | convolution fusion | flops 7531790336 | bytes 40632320 | tf_op jit(solution)/shard_map/dot_general | solution.py:30
  28.6 0.0 all-gather.5.cloned.1.call-start
  28.6 0.7 all-gather.5.cloned.1.call-update
  29.3 0.8 copy-done.1
  30.2 2.5 copy.25
  32.7 4.6 %all-to-all-start = ((bf16[8,512,256]{2,1,0:T(8,128)(2,1)}), bf16[8,512,256]{2,1,0:T(8,128)(2,1)S(1)}, u32[]{:S(2)}, u32[]{:S(2)}) async-start(bf16[8,512,256]{2,1,0:T(8,128)(2,1)} %bitcast.18), calls=%async_computation | async-start | bytes 4194304 | tf_op jit(solution)/shard_map/all_to_all | solution.py:29
  37.2 8.9 %copy.27 = f32[512,3584]{0,1:T(8,128)} copy(f32[512,3584]{1,0:T(8,128)} %param.13) | data formatting | bytes 14680064 | tf_op args[6]
  46.1 8.4 %copy.24 = f32[512,3584]{0,1:T(8,128)} copy(f32[512,3584]{1,0:T(8,128)} %param.12) | data formatting | bytes 14680064 | tf_op args[5]
  54.5 4.1 %constant_dynamic-slice_fusion = bf16[512,3584]{1,0:T(8,128)(2,1)} fusion(bf16[4096,3584]{1,0:T(8,128)(2,1)} %param.11, s32[]{:T(128)S(6)} %select_n.47), kind=kLoop, calls=%fused_computation.54 | loop fusion | bytes 7340036 | tf_op jit(solution)/shard_map/dynamic_slice | solution.py:47
  58.5 6.0 %copy.32 = bf16[512,3584]{0,1:T(8,128)(2,1)} copy(bf16[512,3584]{1,0:T(8,128)(2,1)} %constant_dynamic-slice_fusion) | data formatting | bytes 7340032
  64.5 15.2 %all-to-all-done = bf16[8,512,256]{2,1,0:T(8,128)(2,1)S(1)} async-done(((bf16[8,512,256]{2,1,0:T(8,128)(2,1)}), bf16[8,512,256]{2,1,0:T(8,128)(2,1)S(1)}, u32[]{:S(2)}, u32[]{:S(2)}) %all-to-all-start) | async-done | bytes 2097184 | tf_op jit(solution)/shard_map/all_to_all | solution.py:29
  79.7 2.4 copy.26
  82.1 49.7 %all-gather.3.cloned.1.call-done = bf16[2048,3584]{1,0:T(8,128)(2,1)} async-done(((bf16[256,3584]{1,0:T(8,128)(2,1)}), bf16[2048,3584]{1,0:T(8,128)(2,1)}) %all-gather.3.cloned.1.call-update) | async-done | bytes 14680080 | tf_op jit(solution)/shard_map/all_gather | solution.py:27
  131.8 4.7 %convolution_convert_fusion = bf16[3584,512]{1,0:T(8,128)(2,1)} fusion(bf16[2048,3584]{1,0:T(8,128)(2,1)} %all-gather.3.cloned.1.call-done, bf16[512,2048]{0,1:T(8,128)(2,1)} %bitcast.19), kind=kOutput, calls=%fused_computation.10 | convolution fusion | flops 941359104 | bytes 5767168 | tf_op jit(solution)/shard_map/dot_general | solution.py:37
  136.5 5.3 %convolution_convert_fusion.1 = bf16[3584,512]{1,0:T(8,128)(2,1)} fusion(bf16[2048,3584]{1,0:T(8,128)(2,1)} %all-gather.3.cloned.1.call-done, bf16[512,2048]{0,1:T(8,128)(2,1)S(1)} %bitcast.20), kind=kOutput, calls=%fused_computation.11 | convolution fusion | flops 941359104 | bytes 5767168 | tf_op jit(solution)/shard_map/dot_general | solution.py:37
  141.8 2.9 convolution_convert_fusion.2
  144.8 3.1 convolution_convert_fusion.3
  147.8 3.0 convolution_convert_fusion.4
  150.8 2.9 convolution_convert_fusion.5
  153.8 3.0 convolution_convert_fusion.6
  156.7 20.0 %fusion.3 = (f32[512,3584]{0,1:T(8,128)}, f32[512,3584]{0,1:T(8,128)}) fusion(f32[512,3584]{0,1:T(8,128)} %copy.27, f32[512,3584]{0,1:T(8,128)} %copy.24, bf16[3584,512]{1,0:T(8,128)(2,1)} %convolution_convert_fusion, bf16[3584,512]{1,0:T(8,128)(2,1)} %convolution_convert_fusion.1, bf16[3584,512]{1,0:T(8,128)(2,1)} %convolution_convert_fusion.2, ...), kind=kOutput, calls=%fused_computation.6 | convolution fusion | flops 981729280 | bytes 57147392 | tf_op jit(solution)/shard_map/dot_general | solution.py:37
  176.8 38.0 %all-gather.5.cloned.1.call-done = bf16[2048,3584]{1,0:T(8,128)(2,1)} async-done(((bf16[256,3584]{1,0:T(8,128)(2,1)}), bf16[2048,3584]{1,0:T(8,128)(2,1)}) %all-gather.5.cloned.1.call-update) | async-done | bytes 14680080 | tf_op jit(solution)/shard_map/all_gather | solution.py:28
  214.7 25.4 %fusion.13 = f32[512,2048]{1,0:T(8,128)} fusion(bf16[2048,3584]{1,0:T(8,128)(2,1)} %all-gather.5.cloned.1.call-done, bf16[512,3584]{0,1:T(8,128)(2,1)} %copy.32, f32[512,3584]{0,1:T(8,128)} %get-tuple-element.20, f32[512,3584]{0,1:T(8,128)} %get-tuple-element.21), kind=kOutput, calls=%fused_computation.32 | convolution fusion | flops 7534542848 | bytes 37224448 | tf_op jit(solution)/shard_map/dot_general | solution.py:55
  240.2 76.5 %reduce-scatter.2.cloned.1.call-done = f32[512,512]{1,0:T(8,128)} async-done(((f32[512,2048]{1,0:T(8,128)}), f32[512,512]{1,0:T(8,128)}) %reduce-scatter.2.cloned.1.call-update) | async-done | bytes 1048592 | tf_op jit(solution)/shard_map/reduce_scatter | solution.py:59
  316.7 1.3 convert_element_type.126
  318.0 1.8 collective-permute-start
  319.8 3.1 collective-permute-start.1
  322.9 8.4 %copy.29 = f32[512,3584]{1,0:T(8,128)} copy(f32[512,3584]{0,1:T(8,128)} %get-tuple-element.21) | data formatting | bytes 14680064
  331.3 8.4 %copy.30 = f32[512,3584]{1,0:T(8,128)} copy(f32[512,3584]{0,1:T(8,128)} %get-tuple-element.20) | data formatting | bytes 14680064
  339.6 10.6 %collective-permute-done = bf16[256,512]{0,1:T(8,128)(2,1)S(1)} collective-permute-done((bf16[256,512]{0,1:T(8,128)(2,1)S(1)}, bf16[256,512]{0,1:T(8,128)(2,1)S(1)}, u32[]{:S(2)}, u32[]{:S(2)}) %collective-permute-start) | collective-permute-done | bytes 262176 | tf_op jit(solution)/shard_map/ppermute | solution.py:74
  350.2 5.6 %collective-permute-done.1 = bf16[256,512]{0,1:T(8,128)(2,1)S(1)} collective-permute-done((bf16[256,512]{0,1:T(8,128)(2,1)S(1)}, bf16[256,512]{0,1:T(8,128)(2,1)S(1)}, u32[]{:S(2)}, u32[]{:S(2)}) %collective-permute-start.1) | collective-permute-done | bytes 262176 | tf_op jit(solution)/shard_map/ppermute | solution.py:74
  355.9 1.0 copy.31
  (12 shorter events, 0.2 us)
Async XLA Ops:
  7.2 124.7 %all-gather.3.cloned.1.call-start = ((), (), s32[]{:S(2)}) async-start(), calls=%async_computation.2 | async-start | bytes 16515072 | tf_op jit(solution)/shard_map/all_gather | solution.py:27
  28.6 1.6 copy-start.1
  28.6 186.1 %all-gather.5.cloned.1.call-start = ((), (), s32[]{:S(2)}) async-start(), calls=%async_computation.3 | async-start | bytes 16515072 | tf_op jit(solution)/shard_map/all_gather | solution.py:28
  32.7 47.1 %all-to-all-start = ((bf16[8,512,256]{2,1,0:T(8,128)(2,1)}), bf16[8,512,256]{2,1,0:T(8,128)(2,1)S(1)}, u32[]{:S(2)}, u32[]{:S(2)}) async-start(bf16[8,512,256]{2,1,0:T(8,128)(2,1)} %bitcast.18), calls=%async_computation | async-start | bytes 4194304 | tf_op jit(solution)/shard_map/all_to_all | solution.py:29
  37.2 279.4 %reduce-scatter.2.cloned.1.call-start = ((), (), s32[]{:S(2)}) async-start(), calls=%async_computation.4 | async-start | bytes 5242880 | tf_op jit(solution)/shard_map/reduce_scatter | solution.py:59
  131.8 4.7 %copy-start = (bf16[512,8,256]{0,2,1:T(8,128)(2,1)S(1)}, bf16[512,8,256]{0,2,1:T(8,128)(2,1)}, u32[]{:S(2)}) copy-start(bf16[512,8,256]{0,2,1:T(8,128)(2,1)} %copy.26) | copy-start | bytes 6291460
  131.8 10.0 %copy-start.2 = (bf16[2048,3584]{1,0:T(8,128)(2,1)S(1)}, bf16[2048,3584]{1,0:T(8,128)(2,1)}, u32[]{:S(2)}) copy-start(bf16[2048,3584]{1,0:T(8,128)(2,1)} %all-gather.3.cloned.1.call-done) | copy-start | bytes 44040196
  318.0 32.2 %collective-permute-start = (bf16[256,512]{0,1:T(8,128)(2,1)S(1)}, bf16[256,512]{0,1:T(8,128)(2,1)S(1)}, u32[]{:S(2)}, u32[]{:S(2)}) collective-permute-start(bf16[256,512]{0,1:T(8,128)(2,1)S(1)} %get-tuple-element.28), channel_id=1, source_target_pairs={{0,4},{1,12},{2,20},{3,28},{4,0},{5,8},{6,16},{7,24},{8,5},{9,13},... | collective-permute-start | bytes 786440 | tf_op jit(solution)/shard_map/ppermute | solution.py:74
  319.8 36.1 %collective-permute-start.1 = (bf16[256,512]{0,1:T(8,128)(2,1)S(1)}, bf16[256,512]{0,1:T(8,128)(2,1)S(1)}, u32[]{:S(2)}, u32[]{:S(2)}) collective-permute-start(bf16[256,512]{0,1:T(8,128)(2,1)S(1)} %get-tuple-element.27), channel_id=1, source_target_pairs={{0,0},{1,8},{2,16},{3,24},{4,4},{5,12},{6,20},{7,28},{8,1},{9,9},{... | collective-permute-start | bytes 786440 | tf_op jit(solution)/shard_map/ppermute | solution.py:74
Sparse Core Ops, SparseCore 0:
  28.7 103.0 all-gather.2
  133.7 80.9 all-gather.4
  240.2 76.3 reduce-scatter.1
where the time goes:
time: 364 us; the launch traced here: 363 us
  waiting for transfers between devices  196 us (54%)
  matrix products  91.7 us (25%)
  local copies, waits for them, and re-layouts  50.8 us (14%)
  between operations  13.8 us (4%)
  starting transfers between devices  9.51 us (3%)
    reduce_scatter x1, waiting for transfers between devices, shards(): lax.psum_scatter(partial_out, 'tensor', scatter_dimension=1, tiled=True)  76.5 us
    all_gather x1, waiting for transfers between devices, shards(): hidden_all = lax.all_gather(hidden, 'dp', axis=0, tiled=True)  49.7 us
    dot_general x8, matrix products, shards(): jnp.dot(grad_rows[:, b * tok:(b + 1) * tok], hidden_all[b * tok:(b + 1) *...  44.9 us
    unnamed x13, local copies, waits for them, and re-layouts  44.3 us
    all_gather x1, waiting for transfers between devices, shards(): next_all = lax.all_gather(next_hidden, 'dp', axis=0, tiled=True)  38 us
    dot_general x1, matrix products, shards(): lax.dot_general(new_shard, next_all, (((1,), (1,)), ((), ())), preferred_...  25.4 us
    dot_general x1, matrix products, shards(): jnp.dot(grad_out, down_weight, preferred_element_type=jnp.float32)  21.4 us
    ppermute x2, waiting for transfers between devices, shards(): pieces.append(lax.ppermute(piece, ('dp', 'tensor'), perm))  16.2 us
  transfers between devices with their start and end apart: 6, of which 6 were waited for; matrix products, arithmetic and copies ran while one was open for 26% of the time, Pallas kernels for 0%

commit v1 on v0

--- a/solution.py
+++ b/solution.py
@@ -25,7 +25,25 @@
     activated = gate_value * sigmoid_gate
     hidden = (activated * up_value).astype(jnp.bfloat16)
     hidden_all = lax.all_gather(hidden, "dp", axis=0, tiled=True)
-    next_all = lax.all_gather(next_hidden, "dp", axis=0, tiled=True)
+    length, place, rows = (lax.axis_size("dp"), lax.axis_index("dp"), next_hidden.shape[0])
+    ahead = [(i_2, (i_2 + 1) % length) for i_2 in range(length)]
+    left = [(i_2, (i_2 - 1) % length) for i_2 in range(length)]
+    next_all = jnp.zeros(
+        (*next_hidden.shape[:0], length * rows, *next_hidden.shape[0 + 1 :]), next_hidden.dtype
+    )
+    next_all = lax.dynamic_update_slice_in_dim(next_all, next_hidden, place * rows, axis=0)
+    from_left = from_right = next_hidden
+    half = length // 2
+    for step in range(1, half + 1):
+        from_left = lax.ppermute(from_left, "dp", ahead)
+        next_all = lax.dynamic_update_slice_in_dim(
+            next_all, from_left, (place - step) % length * rows, axis=0
+        )
+        if step < length - half:
+            from_right = lax.ppermute(from_right, "dp", left)
+            next_all = lax.dynamic_update_slice_in_dim(
+                next_all, from_right, (place + step) % length * rows, axis=0
+            )
     grad_rows = lax.all_to_all(grad_out.T, "dp", 0, 1, tiled=True)
     grad_hidden = jnp.dot(grad_out, down_weight, preferred_element_type=jnp.float32)
     gate_grad = (

time: 364 us -> 448 us (1.23)
  waiting for transfers between devices: 196 us -> 244 us
  local copies, waits for them, and re-layouts: 50.8 us -> 75.9 us
  starting transfers between devices: 9.51 us -> 20.5 us
    ppermute x0 -> x7, waiting for transfers between devices: none -> 149 us  [the longest x4 148 us: shards(): from_left = lax.ppermute(from_left, 'dp', ahead)]
    all_gather x1, waiting for transfers between devices: 49.7 us -> 0.01 us  [shards(): hidden_all = lax.all_gather(hidden, 'dp', axis=0, tiled=True)]
    all_gather x1 -> x0, waiting for transfers between devices: 38 us -> none  [shards(): next_all = lax.all_gather(next_hidden, 'dp', axis=0, tiled=True)]
    dynamic_update_slice x0 -> x8, local copies, waits for them, and re-layouts: none -> 20.1 us  [the longest x4 9.96 us: shards(): lax.dynamic_update_slice_in_dim(next_all, from_left, (place - step) % len...]
    all_to_all x1, waiting for transfers between devices: 15.2 us -> 0.1 us  [shards(): grad_rows = lax.all_to_all(grad_out.T, 'dp', 0, 1, tiled=True)]
    ppermute x0 -> x7, starting transfers between devices: none -> 12 us  [the longest x4 12 us: shards(): from_left = lax.ppermute(from_left, 'dp', ahead)]
    broadcast_in_dim x0 -> x1, local copies, waits for them, and re-layouts: none -> 6.11 us  [shards(): jnp.zeros((*next_hidden.shape[:0], length * rows, *next_hidden.shape[0 +...]
  transfers between devices with their start and end apart: 6 -> 12, of which waited for: 6 -> 9; matrix products, arithmetic and copies ran while one was open for 26% -> 17% of each run, Pallas kernels for 0% -> 0%
where the time goes in v1:
time: 448 us
  waiting for transfers between devices  244 us (54%)
  matrix products  91.3 us (20%)
  local copies, waits for them, and re-layouts  75.9 us (17%)
  starting transfers between devices  20.5 us (5%)
  between operations  14.3 us (3%)
    ppermute x4, waiting for transfers between devices, shards(): from_left = lax.ppermute(from_left, 'dp', ahead)  148 us
    reduce_scatter x1, waiting for transfers between devices, shards(): lax.psum_scatter(partial_out, 'tensor', scatter_dimension=1, tiled=True)  78.7 us
    dot_general x8, matrix products, shards(): jnp.dot(grad_rows[:, b * tok:(b + 1) * tok], hidden_all[b * tok:(b + 1) *...  44.4 us
    unnamed x13, local copies, waits for them, and re-layouts  43.1 us
    dot_general x1, matrix products, shards(): lax.dot_general(new_shard, next_all, (((1,), (1,)), ((), ())), preferred_...  25.5 us
    dot_general x1, matrix products, shards(): jnp.dot(grad_out, down_weight, preferred_element_type=jnp.float32)  21.4 us
    ppermute x2, waiting for transfers between devices, shards(): pieces.append(lax.ppermute(piece, ('dp', 'tensor'), perm))  16.2 us
    ppermute x4, starting transfers between devices, shards(): from_left = lax.ppermute(from_left, 'dp', ahead)  12 us
  transfers between devices with their start and end apart: 12, of which 9 were waited for; matrix products, arithmetic and copies ran while one was open for 17% of the time, Pallas kernels for 0%

profile of v1, /device:TPU:3, one launch (start us, length us, event | category | flops | bytes accessed | tf_op | source)
XLA Modules:
  0.0 447.5 jit_solution(9434962720021613267)
XLA Ops:
  7.2 21.4 %multiply_convert_fusion = (bf16[256,3584]{1,0:T(8,128)(2,1)}, bf16[256,3584]{1,0:T(8,128)(2,1)}, bf16[256,3584]{1,0:T(8,128)(2,1)}) fusion(bf16[256,3584]{1,0:T(8,128)(2,1)} %param.8, bf16[256,3584]{1,0:T(8,128)(2,1)} %param.9, bf16[256,4096]{1,0:T(8,128)(2,1)} %param.7, bf16[4096,3584]{1,0:T(8,128)(2,1)} %param.11), kind=kOutput, calls=%fused_computation.31 | convolution fusion | flops 7531790336 | bytes 40632320 | tf_op jit(solution)/shard_map/dot_general | solution.py:48
  30.5 61.3 %collective-permute-done = bf16[256,3584]{1,0:T(8,128)(2,1)} collective-permute-done((bf16[256,3584]{1,0:T(8,128)(2,1)}, bf16[256,3584]{1,0:T(8,128)(2,1)}, u32[]{:S(2)}, u32[]{:S(2)}) %collective-permute-start) | collective-permute-done | bytes 1835040 | tf_op jit(solution)/shard_map/ppermute | solution.py:38
  91.8 3.4 collective-permute-start.2
  97.7 3.6 all-to-all-start
  101.5 8.5 %copy.27 = f32[512,3584]{0,1:T(8,128)} copy(f32[512,3584]{1,0:T(8,128)} %param.13) | data formatting | bytes 14680064 | tf_op args[6]
  110.0 8.4 %copy.24 = f32[512,3584]{0,1:T(8,128)} copy(f32[512,3584]{1,0:T(8,128)} %param.12) | data formatting | bytes 14680064 | tf_op args[5]
  118.4 48.5 %collective-permute-done.2 = bf16[256,3584]{1,0:T(8,128)(2,1)} collective-permute-done((bf16[256,3584]{1,0:T(8,128)(2,1)}, bf16[256,3584]{1,0:T(8,128)(2,1)}, u32[]{:S(2)}, u32[]{:S(2)}) %collective-permute-start.2) | collective-permute-done | bytes 1835040 | tf_op jit(solution)/shard_map/ppermute | solution.py:38
  166.9 3.4 collective-permute-start.4
  170.3 4.1 constant_dynamic-slice_fusion
  174.4 5.9 %copy.32 = bf16[512,3584]{0,1:T(8,128)(2,1)} copy(bf16[512,3584]{1,0:T(8,128)(2,1)} %constant_dynamic-slice_fusion) | data formatting | bytes 7340032
  180.3 6.1 %broadcast_in_dim.3 = bf16[2048,3584]{1,0:T(8,128)(2,1)} broadcast(bf16[]{:T(256)} %constant.102.clone.1), dimensions={} | broadcast | bytes 14680066 | tf_op jit(solution)/shard_map/broadcast_in_dim | solution.py:31
  195.8 2.9 constant_dynamic-update-slice_fusion.5
  198.7 26.3 %collective-permute-done.4 = bf16[256,3584]{1,0:T(8,128)(2,1)} collective-permute-done((bf16[256,3584]{1,0:T(8,128)(2,1)}, bf16[256,3584]{1,0:T(8,128)(2,1)}, u32[]{:S(2)}, u32[]{:S(2)}) %collective-permute-start.4) | collective-permute-done | bytes 1835040 | tf_op jit(solution)/shard_map/ppermute | solution.py:38
  225.0 3.4 collective-permute-start.6
  228.4 2.9 constant_dynamic-update-slice_fusion.4
  231.3 3.1 constant_dynamic-update-slice_fusion.3
  238.6 11.8 %collective-permute-done.6 = bf16[256,3584]{1,0:T(8,128)(2,1)S(1)} collective-permute-done((bf16[256,3584]{1,0:T(8,128)(2,1)}, bf16[256,3584]{1,0:T(8,128)(2,1)S(1)}, u32[]{:S(2)}, u32[]{:S(2)}) %collective-permute-start.6) | collective-permute-done | bytes 1835040 | tf_op jit(solution)/shard_map/ppermute | solution.py:38
  251.8 4.7 %convolution_convert_fusion = bf16[3584,512]{1,0:T(8,128)(2,1)} fusion(bf16[2048,3584]{1,0:T(8,128)(2,1)} %all-gather.2.cloned.1.call-done, bf16[512,2048]{0,1:T(8,128)(2,1)S(1)} %bitcast.19), kind=kOutput, calls=%fused_computation.10 | convolution fusion | flops 941359104 | bytes 5767168 | tf_op jit(solution)/shard_map/dot_general | solution.py:55
  256.5 5.3 %convolution_convert_fusion.1 = bf16[3584,512]{1,0:T(8,128)(2,1)} fusion(bf16[2048,3584]{1,0:T(8,128)(2,1)} %all-gather.2.cloned.1.call-done, bf16[512,2048]{0,1:T(8,128)(2,1)S(1)} %bitcast.20), kind=kOutput, calls=%fused_computation.11 | convolution fusion | flops 941359104 | bytes 5767168 | tf_op jit(solution)/shard_map/dot_general | solution.py:55
  261.8 2.9 convolution_convert_fusion.2
  264.7 3.1 convolution_convert_fusion.3
  267.8 3.0 convolution_convert_fusion.4
  270.8 3.0 convolution_convert_fusion.5
  273.7 3.0 convolution_convert_fusion.6
  276.7 19.4 %fusion.3 = (f32[512,3584]{0,1:T(8,128)}, f32[512,3584]{0,1:T(8,128)}) fusion(f32[512,3584]{0,1:T(8,128)} %copy.27, f32[512,3584]{0,1:T(8,128)} %copy.24, bf16[3584,512]{1,0:T(8,128)(2,1)} %convolution_convert_fusion, bf16[3584,512]{1,0:T(8,128)(2,1)} %convolution_convert_fusion.1, bf16[3584,512]{1,0:T(8,128)(2,1)} %convolution_convert_fusion.2, ...), kind=kOutput, calls=%fused_computation.6 | convolution fusion | flops 981729280 | bytes 57147392 | tf_op jit(solution)/shard_map/dot_general | solution.py:55
  296.1 25.5 %fusion.13 = f32[512,2048]{1,0:T(8,128)} fusion(bf16[2048,3584]{1,0:T(8,128)(2,1)} %constant_dynamic-update-slice_fusion, bf16[512,3584]{0,1:T(8,128)(2,1)} %copy.32, f32[512,3584]{0,1:T(8,128)} %get-tuple-element.20, f32[512,3584]{0,1:T(8,128)} %get-tuple-element.21), kind=kOutput, calls=%fused_computation.32 | convolution fusion | flops 7534542848 | bytes 37224448 | tf_op jit(solution)/shard_map/dot_general | solution.py:73
  321.7 78.7 %reduce-scatter.2.cloned.1.call-done = f32[512,512]{1,0:T(8,128)} async-done(((f32[512,2048]{1,0:T(8,128)}), f32[512,512]{1,0:T(8,128)}) %reduce-scatter.2.cloned.1.call-update) | async-done | bytes 1048592 | tf_op jit(solution)/shard_map/reduce_scatter | solution.py:77
  403.6 3.0 collective-permute-start.8
  406.7 8.4 %copy.29 = f32[512,3584]{1,0:T(8,128)} copy(f32[512,3584]{0,1:T(8,128)} %get-tuple-element.21) | data formatting | bytes 14680064
  415.0 8.4 %copy.30 = f32[512,3584]{1,0:T(8,128)} copy(f32[512,3584]{0,1:T(8,128)} %get-tuple-element.20) | data formatting | bytes 14680064
  423.4 10.6 %collective-permute-done.7 = bf16[256,512]{0,1:T(8,128)(2,1)S(1)} collective-permute-done((bf16[256,512]{0,1:T(8,128)(2,1)S(1)}, bf16[256,512]{0,1:T(8,128)(2,1)S(1)}, u32[]{:S(2)}, u32[]{:S(2)}) %collective-permute-start.7) | collective-permute-done | bytes 262176 | tf_op jit(solution)/shard_map/ppermute | solution.py:92
  434.0 5.6 %collective-permute-done.8 = bf16[256,512]{0,1:T(8,128)(2,1)S(1)} collective-permute-done((bf16[256,512]{0,1:T(8,128)(2,1)S(1)}, bf16[256,512]{0,1:T(8,128)(2,1)S(1)}, u32[]{:S(2)}, u32[]{:S(2)}) %collective-permute-start.8) | collective-permute-done | bytes 262176 | tf_op jit(solution)/shard_map/ppermute | solution.py:92
  (32 shorter events, 23.7 us)
Async XLA Ops:
  7.2 88.0 %copy-start.1 = (bf16[256,4096]{1,0:T(8,128)(2,1)S(1)}, bf16[256,4096]{1,0:T(8,128)(2,1)}, u32[]{:S(2)}) copy-start(bf16[256,4096]{1,0:T(8,128)(2,1)} %param.7) | copy-start | bytes 6291460
  7.2 244.6 %all-gather.2.cloned.1.call-start = ((), (), s32[]{:S(2)}) async-start(), calls=%async_computation.2 | async-start | bytes 16515072 | tf_op jit(solution)/shard_map/all_gather | solution.py:27
  28.7 63.1 %collective-permute-start = (bf16[256,3584]{1,0:T(8,128)(2,1)}, bf16[256,3584]{1,0:T(8,128)(2,1)}, u32[]{:S(2)}, u32[]{:S(2)}) collective-permute-start(bf16[256,3584]{1,0:T(8,128)(2,1)} %param.10), channel_id=1, source_target_pairs={{0,4},{4,8},{8,12},{12,16},{16,20},{20,24},{24,28},{28,0},{1,5},{5... | collective-permute-start | bytes 5505032 | tf_op jit(solution)/shard_map/ppermute | solution.py:38
  30.5 70.8 %collective-permute-start.1 = (bf16[256,3584]{1,0:T(8,128)(2,1)}, bf16[256,3584]{1,0:T(8,128)(2,1)}, u32[]{:S(2)}, u32[]{:S(2)}) collective-permute-start(bf16[256,3584]{1,0:T(8,128)(2,1)} %param.10), channel_id=1, source_target_pairs={{0,28},{4,0},{8,4},{12,8},{16,12},{20,16},{24,20},{28,24},{1,29},{... | collective-permute-start | bytes 5505032 | tf_op jit(solution)/shard_map/ppermute | solution.py:43
  91.8 75.1 %collective-permute-start.2 = (bf16[256,3584]{1,0:T(8,128)(2,1)}, bf16[256,3584]{1,0:T(8,128)(2,1)}, u32[]{:S(2)}, u32[]{:S(2)}) collective-permute-start(bf16[256,3584]{1,0:T(8,128)(2,1)} %collective-permute-done), channel_id=1, source_target_pairs={{0,4},{4,8},{8,12},{12,16},{16,20},{20,24},{24,28},{28,0},{1,5},{5... | collective-permute-start | bytes 5505032 | tf_op jit(solution)/shard_map/ppermute | solution.py:38
  97.7 91.7 %all-to-all-start = ((bf16[8,512,256]{2,1,0:T(8,128)(2,1)}), bf16[8,512,256]{2,1,0:T(8,128)(2,1)S(1)}, u32[]{:S(2)}, u32[]{:S(2)}) async-start(bf16[8,512,256]{2,1,0:T(8,128)(2,1)} %bitcast.18), calls=%async_computation | async-start | bytes 4194304 | tf_op jit(solution)/shard_map/all_to_all | solution.py:47
  101.3 299.2 %reduce-scatter.2.cloned.1.call-start = ((), (), s32[]{:S(2)}) async-start(), calls=%async_computation.3 | async-start | bytes 5242880 | tf_op jit(solution)/shard_map/reduce_scatter | solution.py:77
  101.3 94.5 %collective-permute-start.3 = (bf16[256,3584]{1,0:T(8,128)(2,1)}, bf16[256,3584]{1,0:T(8,128)(2,1)}, u32[]{:S(2)}, u32[]{:S(2)}) collective-permute-start(bf16[256,3584]{1,0:T(8,128)(2,1)} %collective-permute-done.1), channel_id=1, source_target_pairs={{0,28},{4,0},{8,4},{12,8},{16,12},{20,16},{24,20},{28,24},{1,29},{... | collective-permute-start | bytes 5505032 | tf_op jit(solution)/shard_map/ppermute | solution.py:43
  166.9 58.1 %collective-permute-start.4 = (bf16[256,3584]{1,0:T(8,128)(2,1)}, bf16[256,3584]{1,0:T(8,128)(2,1)}, u32[]{:S(2)}, u32[]{:S(2)}) collective-permute-start(bf16[256,3584]{1,0:T(8,128)(2,1)} %collective-permute-done.2), channel_id=1, source_target_pairs={{0,4},{4,8},{8,12},{12,16},{16,20},{20,24},{24,28},{28,0},{1,5},{5... | collective-permute-start | bytes 5505032 | tf_op jit(solution)/shard_map/ppermute | solution.py:38
  195.8 41.4 %collective-permute-start.5 = (bf16[256,3584]{1,0:T(8,128)(2,1)}, bf16[256,3584]{1,0:T(8,128)(2,1)S(1)}, u32[]{:S(2)}, u32[]{:S(2)}) collective-permute-start(bf16[256,3584]{1,0:T(8,128)(2,1)} %collective-permute-done.3), channel_id=1, source_target_pairs={{0,28},{4,0},{8,4},{12,8},{16,12},{20,16},{24,20},{28,24},{1,29},{... | collective-permute-start | bytes 5505032 | tf_op jit(solution)/shard_map/ppermute | solution.py:43
  225.0 25.4 %collective-permute-start.6 = (bf16[256,3584]{1,0:T(8,128)(2,1)}, bf16[256,3584]{1,0:T(8,128)(2,1)S(1)}, u32[]{:S(2)}, u32[]{:S(2)}) collective-permute-start(bf16[256,3584]{1,0:T(8,128)(2,1)} %collective-permute-done.4), channel_id=1, source_target_pairs={{0,4},{4,8},{8,12},{12,16},{16,20},{20,24},{24,28},{28,0},{1,5},{5... | collective-permute-start | bytes 5505032 | tf_op jit(solution)/shard_map/ppermute | solution.py:38
  231.3 20.5 %copy-start = (bf16[512,8,256]{0,2,1:T(8,128)(2,1)S(1)}, bf16[512,8,256]{0,2,1:T(8,128)(2,1)}, u32[]{:S(2)}) copy-start(bf16[512,8,256]{0,2,1:T(8,128)(2,1)} %copy.26) | copy-start | bytes 6291460
  251.8 10.0 %copy-start.2 = (bf16[2048,3584]{1,0:T(8,128)(2,1)S(1)}, bf16[2048,3584]{1,0:T(8,128)(2,1)}, u32[]{:S(2)}) copy-start(bf16[2048,3584]{1,0:T(8,128)(2,1)} %all-gather.2.cloned.1.call-done) | copy-start | bytes 44040196
  401.8 32.2 %collective-permute-start.7 = (bf16[256,512]{0,1:T(8,128)(2,1)S(1)}, bf16[256,512]{0,1:T(8,128)(2,1)S(1)}, u32[]{:S(2)}, u32[]{:S(2)}) collective-permute-start(bf16[256,512]{0,1:T(8,128)(2,1)S(1)} %get-tuple-element.28), channel_id=1, source_target_pairs={{0,4},{1,12},{2,20},{3,28},{4,0},{5,8},{6,16},{7,24},{8,5},{9,13},... | collective-permute-start | bytes 786440 | tf_op jit(solution)/shard_map/ppermute | solution.py:92
  403.6 36.0 %collective-permute-start.8 = (bf16[256,512]{0,1:T(8,128)(2,1)S(1)}, bf16[256,512]{0,1:T(8,128)(2,1)S(1)}, u32[]{:S(2)}, u32[]{:S(2)}) collective-permute-start(bf16[256,512]{0,1:T(8,128)(2,1)S(1)} %get-tuple-element.27), channel_id=1, source_target_pairs={{0,0},{1,8},{2,16},{3,24},{4,4},{5,12},{6,20},{7,28},{8,1},{9,9},{... | collective-permute-start | bytes 786440 | tf_op jit(solution)/shard_map/ppermute | solution.py:92
Sparse Core Ops, SparseCore 0:
  28.8 136.1 all-gather.1
  321.8 78.6 reduce-scatter.1
